TPU v7x, 512 devices: a whole 4x8x8 slice. The times are simulated.
512 devices in a mesh: section: 4 (over z_hi, core), seq: 32 (over x, y), head: 4 (over z_lo).
Axes of the slice: x: 4, y: 8, z: 8 (z_hi: 2, z_lo: 4; z = z_hi * 4 + z_lo), core: 2. Of those that a mesh axis runs over, the one named last changes fastest.
Arguments:
- query_heads: bfloat16 [4, 6144, 3072], P('section', 'seq', 'head'), may hold values from -6 to 6
- key_heads: bfloat16 [4, 6144, 3072], P('section', 'seq', 'head'), may hold values from -6 to 6
- value_heads: bfloat16 [4, 6144, 3072], P('section', 'seq', 'head'), may hold values from -6 to 6
- stream: bfloat16 [4, 6144, 3072], P('section', 'seq', 'head'), may hold values from -1.5 to 1.5
- out_weight: bfloat16 [4, 3072, 3072], P('section', 'head', 'seq'), may hold values from -0.109375 to 0.109375
- gate_scale: float32 [4, 3072], P('section', 'head'), may hold values from 0.5 to 1.5
- windows: int32 [16, 27], replicated, may hold values from -1 to 15, as said below
Outputs:
- handed: bfloat16 [4, 6144, 3072], P('section', 'seq', 'head')
Inputs may be any that keep to these rules, and one draw needn't show every extreme that they name: `windows`: row t lists, in an order drawn for each row, tile t + dt for every dt in -1, 0, 1 with 0 <= t + dt < 16 and tile t + dt in the same clip as t, and -1 in all its other slots; clips are runs of whole consecutive temporal tiles.
All inputs are finite; a program needn't handle non-finite values.
Results may differ from a plain program's by a relative error of at most 0.012.
Values may be sent and summed in bfloat16 or wider, within the bound.
No kernel may reach another device: no remote copies, remote signals or barrier semaphores. Data moves between devices by JAX's collectives and lax.ppermute only.
A program may use at most 64 MiB of HBM per device.

v0:
```python
from functools import partial
import math
import jax
import jax.numpy as jnp
from jax import lax
from jax.sharding import PartitionSpec as P

HD = 128
SPATIAL = 1


def shifted(block, axis, distance):
    devices = range(lax.axis_size(axis))
    route = [(i - distance, i) for i in devices if i - distance in devices]
    return lax.ppermute(block, axis, route)


def from_behind(value, axis, steps):
    count = lax.axis_size(axis)
    pairs = [(source, (source + steps) % count) for source in range(count)]
    return lax.ppermute(value, axis, pairs)


def split_heads(slab, head_count):
    return slab.reshape(slab.shape[0], head_count, slab.shape[1] // head_count)


def tile_maxima(key_slab, head_count, spatial_count):
    parts = split_heads(key_slab, head_count).astype(jnp.float32)
    lengths = jnp.sqrt(jnp.sum(parts * parts, axis=2))
    return jnp.max(lengths.reshape(spatial_count, -1, head_count), axis=1)


def slab_keep(nearby, slab_tile, in_range, spatial_count, temporal_count):
    first = jnp.clip(slab_tile, 0, temporal_count - 1) * spatial_count
    return lax.dynamic_slice_in_dim(nearby, first, spatial_count, 1) & in_range


def attend(
    running,
    slab_entry,
    keep,
    query_parts,
    row_bound,
    head_count,
    spatial_count,
    tile_rows,
    score_scale,
):
    weighted, summed = running
    row_count = query_parts.shape[0]
    slab_keys = split_heads(slab_entry[0], head_count)
    slab_values = split_heads(slab_entry[1], head_count)
    scores = (
        jnp.einsum("qhd,khd->hqk", query_parts, slab_keys, preferred_element_type=jnp.float32)
        * score_scale
    )
    row_keep = jnp.broadcast_to(
        keep[:, None, :, None], (spatial_count, tile_rows, spatial_count, tile_rows)
    )
    row_keep = row_keep.reshape(row_count, row_count)
    weights = jnp.where(row_keep[None], jnp.exp(scores - row_bound.T[:, :, None]), 0.0)
    summed = summed + jnp.sum(weights, axis=2)
    weighted = weighted + jnp.einsum(
        "hqk,khd->qhd",
        weights.astype(jnp.bfloat16),
        slab_values,
        preferred_element_type=jnp.float32,
    )
    return (weighted, summed)


def on_device(query_heads, key_heads, value_heads, stream, out_weight, gate_scale, windows):
    queries = query_heads[0]
    own_keys = key_heads[0]
    own_values = value_heads[0]
    row_count, feature_count = queries.shape
    head_count = feature_count // HD
    spatial_count = SPATIAL
    tile_rows = row_count // spatial_count
    tile_count = windows.shape[0]
    temporal_count = tile_count // spatial_count
    score_scale = 1.0 / math.sqrt(HD)
    seq_count = lax.axis_size("seq")
    position = lax.axis_index("seq")
    temporal = position // 2
    allowed = jnp.any(
        windows[:, :, None] == jnp.arange(tile_count, dtype=jnp.int32)[None, None, :], axis=1
    )
    nearby = lax.dynamic_slice_in_dim(allowed, temporal * spatial_count, spatial_count, 0)
    always = jnp.array(True)
    slabs = [(own_keys, own_values, temporal, always)]
    reach = min(3, seq_count - 1)
    offsets = list(range(1, reach + 1)) + list(range(-reach, 0))
    for offset in offsets:
        moved_keys, moved_values = shifted((own_keys, own_values), "seq", offset)
        source = position - offset
        in_range = (source >= 0) & (source < seq_count)
        slabs.append((moved_keys, moved_values, source // 2, in_range))
    keeps = [
        slab_keep(nearby, slab_entry[2], slab_entry[3], spatial_count, temporal_count)
        for slab_entry in slabs
    ]
    bound_tiles = jnp.zeros((spatial_count, head_count), jnp.float32)
    for slab_entry, keep in zip(slabs, keeps):
        maxima = tile_maxima(slab_entry[0], head_count, spatial_count)
        candidate = jnp.where(keep[:, :, None], maxima[None, :, :], 0.0)
        bound_tiles = jnp.maximum(bound_tiles, jnp.max(candidate, axis=1))
    query_parts = split_heads(queries, head_count)
    query_float = query_parts.astype(jnp.float32)
    query_lengths = jnp.sqrt(jnp.sum(query_float * query_float, axis=2))
    row_bound = query_lengths * jnp.repeat(bound_tiles, tile_rows, axis=0) * score_scale
    running = (
        jnp.zeros((row_count, head_count, HD), jnp.float32),
        jnp.zeros((head_count, row_count), jnp.float32),
    )
    for slab_entry, keep in zip(slabs, keeps):
        step_fn = partial(
            attend,
            slab_entry=slab_entry,
            keep=keep,
            query_parts=query_parts,
            row_bound=row_bound,
            head_count=head_count,
            spatial_count=spatial_count,
            tile_rows=tile_rows,
            score_scale=score_scale,
        )
        running = step_fn(running)
    weighted, summed = running
    attended = (
        (weighted / summed.T[:, :, None]).astype(jnp.bfloat16).reshape(row_count, feature_count)
    )
    head_terms = jnp.dot(
        attended,
        lax.all_gather(out_weight[0], "seq", axis=1, tiled=True),
        preferred_element_type=jnp.float32,
    )
    mixed = lax.psum_scatter(
        head_terms.astype(jnp.bfloat16), "head", scatter_dimension=1, tiled=True
    ).astype(jnp.float32)
    updated = (stream[0].astype(jnp.float32) + gate_scale[0][None, :] * mixed).astype(jnp.bfloat16)
    handed = from_behind(updated, "section", 1)
    return handed[None]


def solution(mesh):
    in_specs = (
        P("section", "seq", "head"),
        P("section", "seq", "head"),
        P("section", "seq", "head"),
        P("section", "seq", "head"),
        P("section", "head", "seq"),
        P("section", "head"),
        P(),
    )
    out_specs = P("section", "seq", "head")
    return jax.shard_map(
        on_device, mesh=mesh, in_specs=in_specs, out_specs=out_specs, check_vma=False
    )
```

profile of v0, /device:TPU:2, one launch (start us, length us, event | category | flops | bytes accessed | tf_op | source)
XLA Modules:
  0.0 199.8 jit_solution(8086827323401507072)
XLA Ops:
  6.5 0.7 all-gather.3.cloned.1.call-update
  7.3 6.1 %collective-permute-start.4 = (bf16[192,768]{1,0:T(8,128)(2,1)}, bf16[192,768]{1,0:T(8,128)(2,1)S(1)}, u32[]{:S(2)}, u32[]{:S(2)}) collective-permute-start(bf16[192,768]{1,0:T(8,128)(2,1)} %bitcast.145), channel_id=1, source_target_pairs={{8,0},{12,4},{16,8},{20,12},{24,16},{28,20},{32,24},{36,28},{40,32... | collective-permute-start | bytes 884744 | tf_op jit(solution)/shard_map/ppermute | solution.py:15
  13.5 3.3 %collective-permute-start.5 = (bf16[192,768]{1,0:T(8,128)(2,1)}, bf16[192,768]{1,0:T(8,128)(2,1)S(1)}, u32[]{:S(2)}, u32[]{:S(2)}) collective-permute-start(bf16[192,768]{1,0:T(8,128)(2,1)} %bitcast.146), channel_id=1, source_target_pairs={{4,0},{8,4},{12,8},{16,12},{20,16},{24,20},{28,24},{32,28},{36,32}... | collective-permute-start | bytes 884744 | tf_op jit(solution)/shard_map/ppermute | solution.py:15
  16.7 1.9 collective-permute-start.2
  18.7 7.8 %collective-permute-start.3 = (bf16[192,768]{1,0:T(8,128)(2,1)}, bf16[192,768]{1,0:T(8,128)(2,1)}, u32[]{:S(2)}, u32[]{:S(2)}) collective-permute-start(bf16[192,768]{1,0:T(8,128)(2,1)} %bitcast.148), channel_id=1, source_target_pairs={{12,0},{16,4},{20,8},{24,12},{28,16},{32,20},{36,24},{40,28},{44,3... | collective-permute-start | bytes 884744 | tf_op jit(solution)/shard_map/ppermute | solution.py:15
  26.5 2.6 %collective-permute-start = (bf16[192,768]{1,0:T(8,128)(2,1)}, bf16[192,768]{1,0:T(8,128)(2,1)S(1)}, u32[]{:S(2)}, u32[]{:S(2)}) collective-permute-start(bf16[192,768]{1,0:T(8,128)(2,1)} %bitcast.149), channel_id=1, source_target_pairs={{0,4},{4,8},{8,12},{12,16},{16,20},{20,24},{24,28},{28,32},{32,36}... | collective-permute-start | bytes 884744 | tf_op jit(solution)/shard_map/ppermute | solution.py:15
  29.1 1.3 reshape_squeeze.11
  30.4 1.4 reshape_squeeze.10
  32.4 0.4 fusion.75
  33.2 0.4 reshape_squeeze.12
  33.5 0.7 fusion.90
  38.0 2.0 %collective-permute-start.1 = (bf16[192,768]{1,0:T(8,128)(2,1)S(1)}, bf16[192,768]{1,0:T(8,128)(2,1)}, u32[]{:S(2)}, u32[]{:S(2)}) collective-permute-start(bf16[192,768]{1,0:T(8,128)(2,1)S(1)} %bitcast.150), channel_id=1, source_target_pairs={{0,8},{4,12},{8,16},{12,20},{16,24},{20,28},{24,32},{28,36},{32,40... | collective-permute-start | bytes 884744 | tf_op jit(solution)/shard_map/ppermute | solution.py:15
  40.0 0.3 reshape.184
  40.7 2.5 %collective-permute-start.6 = (bf16[192,768]{1,0:T(8,128)(2,1)S(1)}, bf16[192,768]{1,0:T(8,128)(2,1)}, u32[]{:S(2)}, u32[]{:S(2)}) collective-permute-start(bf16[192,768]{1,0:T(8,128)(2,1)S(1)} %bitcast.151), channel_id=1, source_target_pairs={{0,4},{4,8},{8,12},{12,16},{16,20},{20,24},{24,28},{28,32},{32,36}... | collective-permute-start | bytes 884744 | tf_op jit(solution)/shard_map/ppermute | solution.py:15
  43.8 6.9 %collective-permute-start.10 = (bf16[192,768]{1,0:T(8,128)(2,1)S(1)}, bf16[192,768]{1,0:T(8,128)(2,1)}, u32[]{:S(2)}, u32[]{:S(2)}) collective-permute-start(bf16[192,768]{1,0:T(8,128)(2,1)S(1)} %bitcast.152), channel_id=1, source_target_pairs={{8,0},{12,4},{16,8},{20,12},{24,16},{28,20},{32,24},{36,28},{40,32... | collective-permute-start | bytes 884744 | tf_op jit(solution)/shard_map/ppermute | solution.py:15
  51.7 4.7 %collective-permute-done.3 = bf16[192,768]{1,0:T(8,128)(2,1)} collective-permute-done((bf16[192,768]{1,0:T(8,128)(2,1)}, bf16[192,768]{1,0:T(8,128)(2,1)}, u32[]{:S(2)}, u32[]{:S(2)}) %collective-permute-start.3) | collective-permute-done | bytes 294944 | tf_op jit(solution)/shard_map/ppermute | solution.py:15
  56.4 7.9 %collective-permute-start.9 = (bf16[192,768]{1,0:T(8,128)(2,1)S(1)}, bf16[192,768]{1,0:T(8,128)(2,1)}, u32[]{:S(2)}, u32[]{:S(2)}) collective-permute-start(bf16[192,768]{1,0:T(8,128)(2,1)S(1)} %bitcast.153), channel_id=1, source_target_pairs={{12,0},{16,4},{20,8},{24,12},{28,16},{32,20},{36,24},{40,28},{44,3... | collective-permute-start | bytes 884744 | tf_op jit(solution)/shard_map/ppermute | solution.py:15
  64.3 1.3 reshape.183
  65.9 2.2 %collective-permute-start.8 = (bf16[192,768]{1,0:T(8,128)(2,1)S(1)}, bf16[192,768]{1,0:T(8,128)(2,1)S(1)}, u32[]{:S(2)}, u32[]{:S(2)}) collective-permute-start(bf16[192,768]{1,0:T(8,128)(2,1)S(1)} %bitcast.154), channel_id=1, source_target_pairs={{0,12},{4,16},{8,20},{12,24},{16,28},{20,32},{24,36},{28,40},{32,4... | collective-permute-start | bytes 884744 | tf_op jit(solution)/shard_map/ppermute | solution.py:15
  68.9 5.1 %collective-permute-start.11 = (bf16[192,768]{1,0:T(8,128)(2,1)S(1)}, bf16[192,768]{1,0:T(8,128)(2,1)}, u32[]{:S(2)}, u32[]{:S(2)}) collective-permute-start(bf16[192,768]{1,0:T(8,128)(2,1)S(1)} %bitcast.155), channel_id=1, source_target_pairs={{4,0},{8,4},{12,8},{16,12},{20,16},{24,20},{28,24},{32,28},{36,32}... | collective-permute-start | bytes 884744 | tf_op jit(solution)/shard_map/ppermute | solution.py:15
  74.0 1.3 reshape.181
  76.1 0.7 fusion.82
  76.9 1.2 fusion.96
  78.0 0.5 fusion.92
  78.5 0.4 fusion.45
  78.9 1.4 fusion.93
  80.4 0.5 fusion.94
  80.9 2.6 %collective-permute-start.7 = (bf16[192,768]{1,0:T(8,128)(2,1)S(1)}, bf16[192,768]{1,0:T(8,128)(2,1)S(1)}, u32[]{:S(2)}, u32[]{:S(2)}) collective-permute-start(bf16[192,768]{1,0:T(8,128)(2,1)S(1)} %bitcast.156), channel_id=1, source_target_pairs={{0,8},{4,12},{8,16},{12,20},{16,24},{20,28},{24,32},{28,36},{32,40... | collective-permute-start | bytes 884744 | tf_op jit(solution)/shard_map/ppermute | solution.py:15
  83.5 1.4 fusion.37
  84.9 3.7 %collective-permute-done.9 = bf16[192,768]{1,0:T(8,128)(2,1)} collective-permute-done((bf16[192,768]{1,0:T(8,128)(2,1)S(1)}, bf16[192,768]{1,0:T(8,128)(2,1)}, u32[]{:S(2)}, u32[]{:S(2)}) %collective-permute-start.9) | collective-permute-done | bytes 294944 | tf_op jit(solution)/shard_map/ppermute | solution.py:15
  88.6 1.4 fusion.39
  90.0 1.4 fusion.95
  91.4 0.5 fusion.91
  91.9 2.7 %collective-permute-done.8 = bf16[192,768]{1,0:T(8,128)(2,1)S(1)} collective-permute-done((bf16[192,768]{1,0:T(8,128)(2,1)S(1)}, bf16[192,768]{1,0:T(8,128)(2,1)S(1)}, u32[]{:S(2)}, u32[]{:S(2)}) %collective-permute-start.8) | collective-permute-done | bytes 294944 | tf_op jit(solution)/shard_map/ppermute | solution.py:15
  94.6 0.4 fusion.41
  95.2 1.4 fusion.35
  96.5 0.5 fusion.97
  97.1 1.4 convolution_add_fusion.1
  98.4 2.4 %collective-permute-done.7 = bf16[192,768]{1,0:T(8,128)(2,1)S(1)} collective-permute-done((bf16[192,768]{1,0:T(8,128)(2,1)S(1)}, bf16[192,768]{1,0:T(8,128)(2,1)S(1)}, u32[]{:S(2)}, u32[]{:S(2)}) %collective-permute-start.7) | collective-permute-done | bytes 294944 | tf_op jit(solution)/shard_map/ppermute | solution.py:15
  100.9 0.5 fusion.33
  101.3 31.5 %all-gather.3.cloned.1.call-done = bf16[1,768,3072]{1,2,0:T(8,128)(2,1)} async-done(((bf16[1,768,96]{1,2,0:T(8,128)(2,1)}), bf16[1,768,3072]{1,2,0:T(8,128)(2,1)}) %all-gather.3.cloned.1.call-update) | async-done | bytes 4718608 | tf_op jit(solution)/shard_map/all_gather | solution.py:136
  132.8 5.1 %fusion.2 = bf16[192,3072]{1,0:T(8,128)(2,1)} fusion(bf16[1,768,3072]{1,2,0:T(8,128)(2,1)} %all-gather.3.cloned.1.call-done, bf16[6,24,8,128]{3,2,1,0:T(8,128)(2,1)S(1)} %fusion.33), kind=kOutput, calls=%fused_computation.2 | convolution fusion | flops 906559488 | bytes 6193152 | tf_op jit(solution)/shard_map/dot_general | solution.py:134
  137.9 0.7 copy-done.6
  138.6 37.7 %reduce-scatter.2.cloned.1.call-done = bf16[192,768]{1,0:T(8,128)(2,1)} async-done(((bf16[192,3072]{1,0:T(8,128)(2,1)}), bf16[192,768]{1,0:T(8,128)(2,1)}) %reduce-scatter.2.cloned.1.call-update) | async-done | bytes 294928 | tf_op jit(solution)/shard_map/reduce_scatter | solution.py:139
  176.3 1.1 fusion.34
  177.4 1.9 collective-permute-start.12
  179.3 13.0 %collective-permute-done.12 = bf16[192,768]{1,0:T(8,128)(2,1)S(1)} collective-permute-done((bf16[192,768]{1,0:T(8,128)(2,1)S(1)}, bf16[192,768]{1,0:T(8,128)(2,1)S(1)}, u32[]{:S(2)}, u32[]{:S(2)}) %collective-permute-start.12) | collective-permute-done | bytes 294944 | tf_op jit(solution)/shard_map/ppermute | solution.py:21
  192.3 0.7 copy.306
  (50 shorter events, 4.9 us)
Async XLA Ops:
  6.5 126.3 %all-gather.3.cloned.1.call-start = ((), (), s32[]{:S(2)}) async-start(), calls=%async_computation.2 | async-start | bytes 4866048 | tf_op jit(solution)/shard_map/all_gather | solution.py:136
  7.3 169.1 %reduce-scatter.2.cloned.1.call-start = ((), (), s32[]{:S(2)}) async-start(), calls=%async_computation.1 | async-start | bytes 1474560 | tf_op jit(solution)/shard_map/reduce_scatter | solution.py:139
  7.3 25.1 %copy-start.5 = (s32[16,27]{1,0:T(8,128)S(1)}, s32[16,27]{1,0:T(8,128)}, u32[]{:S(2)}) copy-start(s32[16,27]{1,0:T(8,128)} %param.13) | copy-start | bytes 5188
  7.3 30.7 %collective-permute-start.4 = (bf16[192,768]{1,0:T(8,128)(2,1)}, bf16[192,768]{1,0:T(8,128)(2,1)S(1)}, u32[]{:S(2)}, u32[]{:S(2)}) collective-permute-start(bf16[192,768]{1,0:T(8,128)(2,1)} %bitcast.145), channel_id=1, source_target_pairs={{8,0},{12,4},{16,8},{20,12},{24,16},{28,20},{32,24},{36,28},{40,32... | collective-permute-start | bytes 884744 | tf_op jit(solution)/shard_map/ppermute | solution.py:15
  13.5 27.2 %collective-permute-start.5 = (bf16[192,768]{1,0:T(8,128)(2,1)}, bf16[192,768]{1,0:T(8,128)(2,1)S(1)}, u32[]{:S(2)}, u32[]{:S(2)}) collective-permute-start(bf16[192,768]{1,0:T(8,128)(2,1)} %bitcast.146), channel_id=1, source_target_pairs={{4,0},{8,4},{12,8},{16,12},{20,16},{24,20},{28,24},{32,28},{36,32}... | collective-permute-start | bytes 884744 | tf_op jit(solution)/shard_map/ppermute | solution.py:15
  16.7 27.1 %collective-permute-start.2 = (bf16[192,768]{1,0:T(8,128)(2,1)}, bf16[192,768]{1,0:T(8,128)(2,1)S(1)}, u32[]{:S(2)}, u32[]{:S(2)}) collective-permute-start(bf16[192,768]{1,0:T(8,128)(2,1)} %bitcast.147), channel_id=1, source_target_pairs={{0,12},{4,16},{8,20},{12,24},{16,28},{20,32},{24,36},{28,40},{32,4... | collective-permute-start | bytes 884744 | tf_op jit(solution)/shard_map/ppermute | solution.py:15
  18.7 37.7 %collective-permute-start.3 = (bf16[192,768]{1,0:T(8,128)(2,1)}, bf16[192,768]{1,0:T(8,128)(2,1)}, u32[]{:S(2)}, u32[]{:S(2)}) collective-permute-start(bf16[192,768]{1,0:T(8,128)(2,1)} %bitcast.148), channel_id=1, source_target_pairs={{12,0},{16,4},{20,8},{24,12},{28,16},{32,20},{36,24},{40,28},{44,3... | collective-permute-start | bytes 884744 | tf_op jit(solution)/shard_map/ppermute | solution.py:15
  26.5 39.4 %collective-permute-start = (bf16[192,768]{1,0:T(8,128)(2,1)}, bf16[192,768]{1,0:T(8,128)(2,1)S(1)}, u32[]{:S(2)}, u32[]{:S(2)}) collective-permute-start(bf16[192,768]{1,0:T(8,128)(2,1)} %bitcast.149), channel_id=1, source_target_pairs={{0,4},{4,8},{8,12},{12,16},{16,20},{20,24},{24,28},{28,32},{32,36}... | collective-permute-start | bytes 884744 | tf_op jit(solution)/shard_map/ppermute | solution.py:15
  30.4 2.7 %copy-start.2 = (bf16[1,192,768]{2,1,0:T(8,128)(2,1)S(1)}, bf16[1,192,768]{2,1,0:T(8,128)(2,1)}, u32[]{:S(2)}) copy-start(bf16[1,192,768]{2,1,0:T(8,128)(2,1)} %param.9) | copy-start | bytes 884740
  31.8 6.2 %copy-start.1 = (bf16[1,192,768]{2,1,0:T(8,128)(2,1)S(1)}, bf16[1,192,768]{2,1,0:T(8,128)(2,1)}, u32[]{:S(2)}) copy-start(bf16[1,192,768]{2,1,0:T(8,128)(2,1)} %param.8) | copy-start | bytes 884740
  38.0 2.7 %copy-start.3 = (bf16[192,768]{1,0:T(8,128)(2,1)}, bf16[192,768]{1,0:T(8,128)(2,1)S(1)}, u32[]{:S(2)}) copy-start(bf16[192,768]{1,0:T(8,128)(2,1)S(1)} %collective-permute-done.4) | copy-start | bytes 884740
  38.0 30.9 %collective-permute-start.1 = (bf16[192,768]{1,0:T(8,128)(2,1)S(1)}, bf16[192,768]{1,0:T(8,128)(2,1)}, u32[]{:S(2)}, u32[]{:S(2)}) collective-permute-start(bf16[192,768]{1,0:T(8,128)(2,1)S(1)} %bitcast.150), channel_id=1, source_target_pairs={{0,8},{4,12},{8,16},{12,20},{16,24},{20,28},{24,32},{28,36},{32,40... | collective-permute-start | bytes 884744 | tf_op jit(solution)/shard_map/ppermute | solution.py:15
  40.7 56.4 %collective-permute-start.6 = (bf16[192,768]{1,0:T(8,128)(2,1)S(1)}, bf16[192,768]{1,0:T(8,128)(2,1)}, u32[]{:S(2)}, u32[]{:S(2)}) collective-permute-start(bf16[192,768]{1,0:T(8,128)(2,1)S(1)} %bitcast.151), channel_id=1, source_target_pairs={{0,4},{4,8},{8,12},{12,16},{16,20},{20,24},{24,28},{28,32},{32,36}... | collective-permute-start | bytes 884744 | tf_op jit(solution)/shard_map/ppermute | solution.py:15
  43.8 37.1 %collective-permute-start.10 = (bf16[192,768]{1,0:T(8,128)(2,1)S(1)}, bf16[192,768]{1,0:T(8,128)(2,1)}, u32[]{:S(2)}, u32[]{:S(2)}) collective-permute-start(bf16[192,768]{1,0:T(8,128)(2,1)S(1)} %bitcast.152), channel_id=1, source_target_pairs={{8,0},{12,4},{16,8},{20,12},{24,16},{28,20},{32,24},{36,28},{40,32... | collective-permute-start | bytes 884744 | tf_op jit(solution)/shard_map/ppermute | solution.py:15
  56.4 32.2 %collective-permute-start.9 = (bf16[192,768]{1,0:T(8,128)(2,1)S(1)}, bf16[192,768]{1,0:T(8,128)(2,1)}, u32[]{:S(2)}, u32[]{:S(2)}) collective-permute-start(bf16[192,768]{1,0:T(8,128)(2,1)S(1)} %bitcast.153), channel_id=1, source_target_pairs={{12,0},{16,4},{20,8},{24,12},{28,16},{32,20},{36,24},{40,28},{44,3... | collective-permute-start | bytes 884744 | tf_op jit(solution)/shard_map/ppermute | solution.py:15
  65.9 28.6 %collective-permute-start.8 = (bf16[192,768]{1,0:T(8,128)(2,1)S(1)}, bf16[192,768]{1,0:T(8,128)(2,1)S(1)}, u32[]{:S(2)}, u32[]{:S(2)}) collective-permute-start(bf16[192,768]{1,0:T(8,128)(2,1)S(1)} %bitcast.154), channel_id=1, source_target_pairs={{0,12},{4,16},{8,20},{12,24},{16,28},{20,32},{24,36},{28,40},{32,4... | collective-permute-start | bytes 884744 | tf_op jit(solution)/shard_map/ppermute | solution.py:15
  68.9 26.3 %collective-permute-start.11 = (bf16[192,768]{1,0:T(8,128)(2,1)S(1)}, bf16[192,768]{1,0:T(8,128)(2,1)}, u32[]{:S(2)}, u32[]{:S(2)}) collective-permute-start(bf16[192,768]{1,0:T(8,128)(2,1)S(1)} %bitcast.155), channel_id=1, source_target_pairs={{4,0},{8,4},{12,8},{16,12},{20,16},{24,20},{28,24},{32,28},{36,32}... | collective-permute-start | bytes 884744 | tf_op jit(solution)/shard_map/ppermute | solution.py:15
  76.9 1.2 copy-start.4
  80.9 20.0 %collective-permute-start.7 = (bf16[192,768]{1,0:T(8,128)(2,1)S(1)}, bf16[192,768]{1,0:T(8,128)(2,1)S(1)}, u32[]{:S(2)}, u32[]{:S(2)}) collective-permute-start(bf16[192,768]{1,0:T(8,128)(2,1)S(1)} %bitcast.156), channel_id=1, source_target_pairs={{0,8},{4,12},{8,16},{12,20},{16,24},{20,28},{24,32},{28,36},{32,40... | collective-permute-start | bytes 884744 | tf_op jit(solution)/shard_map/ppermute | solution.py:15
  137.9 0.7 copy-start.6
  137.9 38.4 %copy-start = (bf16[1,192,768]{2,1,0:T(8,128)(2,1)S(1)}, bf16[1,192,768]{2,1,0:T(8,128)(2,1)}, u32[]{:S(2)}) copy-start(bf16[1,192,768]{2,1,0:T(8,128)(2,1)} %param.10) | copy-start | bytes 884740
  177.4 14.9 %collective-permute-start.12 = (bf16[192,768]{1,0:T(8,128)(2,1)S(1)}, bf16[192,768]{1,0:T(8,128)(2,1)S(1)}, u32[]{:S(2)}, u32[]{:S(2)}) collective-permute-start(bf16[192,768]{1,0:T(8,128)(2,1)S(1)} %fusion.34), channel_id=1, source_target_pairs={{0,128},{128,256},{256,384},{384,0},{1,129},{129,257},{257,385},{3... | collective-permute-start | bytes 884744 | tf_op jit(solution)/shard_map/ppermute | solution.py:21
Sparse Core Ops, SparseCore 0:
  10.5 122.2 all-gather.2
  138.0 38.2 reduce-scatter.1
where the time goes:
time: 201 us; the launch traced here: 200 us
  waiting for transfers between devices  96.7 us (48%)
  starting transfers between devices  52.9 us (26%)
  matrix products  17.7 us (9%)
  between operations  17.7 us (9%)
  local copies, waits for them, and re-layouts  9.76 us (5%)
  other arithmetic  4.97 us (2%)
    ppermute x12, starting transfers between devices, shifted(): return lax.ppermute(block, axis, route)  51 us
    reduce_scatter x1, waiting for transfers between devices, on_device(): lax.psum_scatter(head_terms.astype(jnp.bfloat16), 'head', scatter_dimensi...  37.7 us
    all_gather x1, waiting for transfers between devices, on_device(): lax.all_gather(out_weight[0], 'seq', axis=1, tiled=True)  31.5 us
    ppermute x12, waiting for transfers between devices, shifted(): return lax.ppermute(block, axis, route)  13.8 us
    ppermute x1, waiting for transfers between devices, from_behind(): return lax.ppermute(value, axis, pairs)  13 us
    dot_general x7, matrix products, attend(): jnp.einsum('hqk,khd->qhd', weights.astype(jnp.bfloat16), slab_values, pre...  6.68 us
    dot_general x7, matrix products, attend(): jnp.einsum('qhd,khd->hqk', query_parts, slab_keys, preferred_element_type...  5.98 us
    dot_general x1, matrix products, on_device(): jnp.dot(attended, lax.all_gather(out_weight[0], 'seq', axis=1, tiled=True...  5.07 us
  transfers between devices with their start and end apart: 15, of which 8 were waited for; matrix products, arithmetic and copies ran while one was open for 12% of the time, Pallas kernels for 0%

commit v1 on v0

--- a/solution.py
+++ b/solution.py
@@ -133,7 +133,9 @@
     )
     head_terms = jnp.dot(
         attended,
-        lax.all_gather(out_weight[0], "seq", axis=1, tiled=True),
+        jnp.concatenate(
+            lax.all_to_all(jnp.stack([out_weight[0]] * lax.axis_size("seq")), "seq", 0, 0), axis=1
+        ),
         preferred_element_type=jnp.float32,
     )
     mixed = lax.psum_scatter(

time: 201 us -> 286 us (1.42)
  the two profiles are of different devices: /device:TPU:2 before, /device:TPU:6 now
where the time goes in v1:
time: 286 us; the launch traced here: 285 us
  waiting for transfers between devices  164 us (57%)
  starting transfers between devices  69.5 us (24%)
  matrix products  17.8 us (6%)
  between operations  17.7 us (6%)
  local copies, waits for them, and re-layouts  11.4 us (4%)
  other arithmetic  4.96 us (2%)
    ppermute x12, waiting for transfers between devices, shifted(): return lax.ppermute(block, axis, route)  108 us
    ppermute x12, starting transfers between devices, shifted(): return lax.ppermute(block, axis, route)  56.9 us
    reduce_scatter x1, waiting for transfers between devices, on_device(): lax.psum_scatter(head_terms.astype(jnp.bfloat16), 'head', scatter_dimensi...  42.4 us
    ppermute x1, waiting for transfers between devices, from_behind(): return lax.ppermute(value, axis, pairs)  13 us
    all_to_all x1, starting transfers between devices, on_device(): lax.all_to_all(jnp.stack([out_weight[0]] * lax.axis_size('seq')), 'seq',...  10.6 us
    dot_general x7, matrix products, attend(): jnp.einsum('hqk,khd->qhd', weights.astype(jnp.bfloat16), slab_values, pre...  6.71 us
    dot_general x7, matrix products, attend(): jnp.einsum('qhd,khd->hqk', query_parts, slab_keys, preferred_element_type...  5.99 us
  transfers between devices with their start and end apart: 15, of which 8 were waited for; matrix products, arithmetic and copies ran while one was open for 8% of the time, Pallas kernels for 0%

profile of v1, /device:TPU:6, one launch (start us, length us, event | category | flops | bytes accessed | tf_op | source)
XLA Modules:
  0.0 284.9 jit_solution(13911816502245838694)
XLA Ops:
  6.5 3.6 %stack.3 = bf16[32,768,96]{1,2,0:T(8,128)(2,1)} broadcast(bf16[768,96]{0,1:T(8,128)(2,1)} %bitcast.157), dimensions={1,2} | broadcast | bytes 4866048 | tf_op jit(solution)/shard_map/stack | solution.py:137
  10.2 10.6 %all-to-all-start = ((bf16[32,768,96]{1,2,0:T(8,128)(2,1)}), bf16[32,768,96]{1,2,0:T(8,128)(2,1)}, u32[]{:S(2)}, u32[]{:S(2)}) async-start(bf16[32,768,96]{1,2,0:T(8,128)(2,1)} %stack.3), calls=%async_computation | async-start | bytes 9437184 | tf_op jit(solution)/shard_map/all_to_all | solution.py:137
  20.8 4.9 %collective-permute-start.5 = (bf16[192,768]{1,0:T(8,128)(2,1)S(1)}, bf16[192,768]{1,0:T(8,128)(2,1)S(1)}, u32[]{:S(2)}, u32[]{:S(2)}) collective-permute-start(bf16[192,768]{1,0:T(8,128)(2,1)S(1)} %bitcast.145), channel_id=1, source_target_pairs={{4,0},{8,4},{12,8},{16,12},{20,16},{24,20},{28,24},{32,28},{36,32}... | collective-permute-start | bytes 884744 | tf_op jit(solution)/shard_map/ppermute | solution.py:15
  25.7 4.3 %collective-permute-start.4 = (bf16[192,768]{1,0:T(8,128)(2,1)S(1)}, bf16[192,768]{1,0:T(8,128)(2,1)}, u32[]{:S(2)}, u32[]{:S(2)}) collective-permute-start(bf16[192,768]{1,0:T(8,128)(2,1)S(1)} %bitcast.146), channel_id=1, source_target_pairs={{8,0},{12,4},{16,8},{20,12},{24,16},{28,20},{32,24},{36,28},{40,32... | collective-permute-start | bytes 884744 | tf_op jit(solution)/shard_map/ppermute | solution.py:15
  30.0 3.4 %collective-permute-start.3 = (bf16[192,768]{1,0:T(8,128)(2,1)S(1)}, bf16[192,768]{1,0:T(8,128)(2,1)S(1)}, u32[]{:S(2)}, u32[]{:S(2)}) collective-permute-start(bf16[192,768]{1,0:T(8,128)(2,1)S(1)} %bitcast.147), channel_id=1, source_target_pairs={{12,0},{16,4},{20,8},{24,12},{28,16},{32,20},{36,24},{40,28},{44,3... | collective-permute-start | bytes 884744 | tf_op jit(solution)/shard_map/ppermute | solution.py:15
  33.3 4.3 %collective-permute-start.2 = (bf16[192,768]{1,0:T(8,128)(2,1)S(1)}, bf16[192,768]{1,0:T(8,128)(2,1)S(1)}, u32[]{:S(2)}, u32[]{:S(2)}) collective-permute-start(bf16[192,768]{1,0:T(8,128)(2,1)S(1)} %bitcast.148), channel_id=1, source_target_pairs={{0,12},{4,16},{8,20},{12,24},{16,28},{20,32},{24,36},{28,40},{32,4... | collective-permute-start | bytes 884744 | tf_op jit(solution)/shard_map/ppermute | solution.py:15
  37.6 3.7 %collective-permute-start.1 = (bf16[192,768]{1,0:T(8,128)(2,1)S(1)}, bf16[192,768]{1,0:T(8,128)(2,1)S(1)}, u32[]{:S(2)}, u32[]{:S(2)}) collective-permute-start(bf16[192,768]{1,0:T(8,128)(2,1)S(1)} %bitcast.149), channel_id=1, source_target_pairs={{0,8},{4,12},{8,16},{12,20},{16,24},{20,28},{24,32},{28,36},{32,40... | collective-permute-start | bytes 884744 | tf_op jit(solution)/shard_map/ppermute | solution.py:15
  41.3 0.3 reshape_squeeze.11
  42.6 0.4 fusion.70
  43.4 0.3 reshape_squeeze.12
  43.8 0.7 fusion.85
  48.2 83.1 %collective-permute-done.5 = bf16[192,768]{1,0:T(8,128)(2,1)S(1)} collective-permute-done((bf16[192,768]{1,0:T(8,128)(2,1)S(1)}, bf16[192,768]{1,0:T(8,128)(2,1)S(1)}, u32[]{:S(2)}, u32[]{:S(2)}) %collective-permute-start.5) | collective-permute-done | bytes 294944 | tf_op jit(solution)/shard_map/ppermute | solution.py:15
  131.3 5.8 %collective-permute-start = (bf16[192,768]{1,0:T(8,128)(2,1)S(1)}, bf16[192,768]{1,0:T(8,128)(2,1)}, u32[]{:S(2)}, u32[]{:S(2)}) collective-permute-start(bf16[192,768]{1,0:T(8,128)(2,1)S(1)} %bitcast.150), channel_id=1, source_target_pairs={{0,4},{4,8},{8,12},{12,16},{16,20},{20,24},{24,28},{28,32},{32,36}... | collective-permute-start | bytes 884744 | tf_op jit(solution)/shard_map/ppermute | solution.py:15
  137.8 8.6 %collective-permute-done.4 = bf16[192,768]{1,0:T(8,128)(2,1)} collective-permute-done((bf16[192,768]{1,0:T(8,128)(2,1)S(1)}, bf16[192,768]{1,0:T(8,128)(2,1)}, u32[]{:S(2)}, u32[]{:S(2)}) %collective-permute-start.4) | collective-permute-done | bytes 294944 | tf_op jit(solution)/shard_map/ppermute | solution.py:15
  146.4 10.8 %collective-permute-start.11 = (bf16[192,768]{1,0:T(8,128)(2,1)S(1)}, bf16[192,768]{1,0:T(8,128)(2,1)}, u32[]{:S(2)}, u32[]{:S(2)}) collective-permute-start(bf16[192,768]{1,0:T(8,128)(2,1)S(1)} %bitcast.151), channel_id=1, source_target_pairs={{4,0},{8,4},{12,8},{16,12},{20,16},{24,20},{28,24},{32,28},{36,32}... | collective-permute-start | bytes 884744 | tf_op jit(solution)/shard_map/ppermute | solution.py:15
  157.3 1.3 reshape.191
  158.8 6.0 %collective-permute-done.3 = bf16[192,768]{1,0:T(8,128)(2,1)S(1)} collective-permute-done((bf16[192,768]{1,0:T(8,128)(2,1)S(1)}, bf16[192,768]{1,0:T(8,128)(2,1)S(1)}, u32[]{:S(2)}, u32[]{:S(2)}) %collective-permute-start.3) | collective-permute-done | bytes 294944 | tf_op jit(solution)/shard_map/ppermute | solution.py:15
  164.8 3.0 %collective-permute-start.10 = (bf16[192,768]{1,0:T(8,128)(2,1)S(1)}, bf16[192,768]{1,0:T(8,128)(2,1)}, u32[]{:S(2)}, u32[]{:S(2)}) collective-permute-start(bf16[192,768]{1,0:T(8,128)(2,1)S(1)} %bitcast.152), channel_id=1, source_target_pairs={{8,0},{12,4},{16,8},{20,12},{24,16},{28,20},{32,24},{36,28},{40,32... | collective-permute-start | bytes 884744 | tf_op jit(solution)/shard_map/ppermute | solution.py:15
  168.7 6.5 %collective-permute-start.9 = (bf16[192,768]{1,0:T(8,128)(2,1)S(1)}, bf16[192,768]{1,0:T(8,128)(2,1)}, u32[]{:S(2)}, u32[]{:S(2)}) collective-permute-start(bf16[192,768]{1,0:T(8,128)(2,1)S(1)} %bitcast.153), channel_id=1, source_target_pairs={{12,0},{16,4},{20,8},{24,12},{28,16},{32,20},{36,24},{40,28},{44,3... | collective-permute-start | bytes 884744 | tf_op jit(solution)/shard_map/ppermute | solution.py:15
  176.0 1.9 collective-permute-start.8
  178.6 1.9 collective-permute-start.6
  180.5 1.3 reshape.187
  182.7 0.6 fusion.77
  183.4 1.1 fusion.91
  184.6 0.5 fusion.86
  185.1 0.4 fusion.40
  185.5 1.4 fusion.87
  186.9 0.5 fusion.88
  187.5 6.5 %collective-permute-start.7 = (bf16[192,768]{1,0:T(8,128)(2,1)S(1)}, bf16[192,768]{1,0:T(8,128)(2,1)S(1)}, u32[]{:S(2)}, u32[]{:S(2)}) collective-permute-start(bf16[192,768]{1,0:T(8,128)(2,1)S(1)} %bitcast.156), channel_id=1, source_target_pairs={{0,8},{4,12},{8,16},{12,20},{16,24},{20,28},{24,32},{28,36},{32,40... | collective-permute-start | bytes 884744 | tf_op jit(solution)/shard_map/ppermute | solution.py:15
  193.9 1.4 fusion.30
  195.3 1.4 fusion.32
  196.7 0.5 fusion.89
  197.1 1.4 fusion.92
  198.6 3.6 %collective-permute-done.9 = bf16[192,768]{1,0:T(8,128)(2,1)} collective-permute-done((bf16[192,768]{1,0:T(8,128)(2,1)S(1)}, bf16[192,768]{1,0:T(8,128)(2,1)}, u32[]{:S(2)}, u32[]{:S(2)}) %collective-permute-start.9) | collective-permute-done | bytes 294944 | tf_op jit(solution)/shard_map/ppermute | solution.py:15
  202.1 1.4 fusion.34
  203.5 1.4 fusion.36
  204.9 0.5 fusion.90
  205.4 5.8 %collective-permute-done.6 = bf16[192,768]{1,0:T(8,128)(2,1)S(1)} collective-permute-done((bf16[192,768]{1,0:T(8,128)(2,1)S(1)}, bf16[192,768]{1,0:T(8,128)(2,1)S(1)}, u32[]{:S(2)}, u32[]{:S(2)}) %collective-permute-start.6) | collective-permute-done | bytes 294944 | tf_op jit(solution)/shard_map/ppermute | solution.py:15
  211.2 0.4 convolution_add_fusion.1
  211.6 1.0 collective-permute-done.7
  212.7 0.5 fusion.28
  213.2 5.1 %convolution_convert_fusion = bf16[192,3072]{1,0:T(8,128)(2,1)} fusion(bf16[768,3072]{0,1:T(8,128)(2,1)} %bitcast.21, bf16[6,24,8,128]{3,2,1,0:T(8,128)(2,1)S(1)} %fusion.28), kind=kOutput, calls=%fused_computation | convolution fusion | flops 906559488 | bytes 6193152 | tf_op jit(solution)/shard_map/dot_general | solution.py:134
  218.3 0.7 copy-done.7
  218.9 42.4 %reduce-scatter.2.cloned.1.call-done = bf16[192,768]{1,0:T(8,128)(2,1)} async-done(((bf16[192,3072]{1,0:T(8,128)(2,1)}), bf16[192,768]{1,0:T(8,128)(2,1)}) %reduce-scatter.2.cloned.1.call-update) | async-done | bytes 294928 | tf_op jit(solution)/shard_map/reduce_scatter | solution.py:141
  261.4 1.1 fusion.29
  262.4 1.9 collective-permute-start.12
  264.3 13.0 %collective-permute-done.12 = bf16[192,768]{1,0:T(8,128)(2,1)S(1)} collective-permute-done((bf16[192,768]{1,0:T(8,128)(2,1)S(1)}, bf16[192,768]{1,0:T(8,128)(2,1)S(1)}, u32[]{:S(2)}, u32[]{:S(2)}) %collective-permute-start.12) | collective-permute-done | bytes 294944 | tf_op jit(solution)/shard_map/ppermute | solution.py:21
  277.3 0.7 copy.307
  (52 shorter events, 5.4 us)
Async XLA Ops:
  10.1 10.6 %copy-start.2 = (bf16[1,192,768]{2,1,0:T(8,128)(2,1)S(1)}, bf16[1,192,768]{2,1,0:T(8,128)(2,1)}, u32[]{:S(2)}) copy-start(bf16[1,192,768]{2,1,0:T(8,128)(2,1)} %param.8) | copy-start | bytes 884740
  10.2 31.5 %copy-start.1 = (bf16[1,192,768]{2,1,0:T(8,128)(2,1)S(1)}, bf16[1,192,768]{2,1,0:T(8,128)(2,1)}, u32[]{:S(2)}) copy-start(bf16[1,192,768]{2,1,0:T(8,128)(2,1)} %param.7) | copy-start | bytes 884740
  10.2 203.0 %all-to-all-start = ((bf16[32,768,96]{1,2,0:T(8,128)(2,1)}), bf16[32,768,96]{1,2,0:T(8,128)(2,1)}, u32[]{:S(2)}, u32[]{:S(2)}) async-start(bf16[32,768,96]{1,2,0:T(8,128)(2,1)} %stack.3), calls=%async_computation | async-start | bytes 9437184 | tf_op jit(solution)/shard_map/all_to_all | solution.py:137
  20.7 240.6 %reduce-scatter.2.cloned.1.call-start = ((), (), s32[]{:S(2)}) async-start(), calls=%async_computation.2 | async-start | bytes 1474560 | tf_op jit(solution)/shard_map/reduce_scatter | solution.py:141
  20.8 21.8 %copy-start.6 = (s32[16,27]{1,0:T(8,128)S(1)}, s32[16,27]{1,0:T(8,128)}, u32[]{:S(2)}) copy-start(s32[16,27]{1,0:T(8,128)} %param.13) | copy-start | bytes 5188
  20.8 110.5 %collective-permute-start.5 = (bf16[192,768]{1,0:T(8,128)(2,1)S(1)}, bf16[192,768]{1,0:T(8,128)(2,1)S(1)}, u32[]{:S(2)}, u32[]{:S(2)}) collective-permute-start(bf16[192,768]{1,0:T(8,128)(2,1)S(1)} %bitcast.145), channel_id=1, source_target_pairs={{4,0},{8,4},{12,8},{16,12},{20,16},{24,20},{28,24},{32,28},{36,32}... | collective-permute-start | bytes 884744 | tf_op jit(solution)/shard_map/ppermute | solution.py:15
  25.7 120.7 %collective-permute-start.4 = (bf16[192,768]{1,0:T(8,128)(2,1)S(1)}, bf16[192,768]{1,0:T(8,128)(2,1)}, u32[]{:S(2)}, u32[]{:S(2)}) collective-permute-start(bf16[192,768]{1,0:T(8,128)(2,1)S(1)} %bitcast.146), channel_id=1, source_target_pairs={{8,0},{12,4},{16,8},{20,12},{24,16},{28,20},{32,24},{36,28},{40,32... | collective-permute-start | bytes 884744 | tf_op jit(solution)/shard_map/ppermute | solution.py:15
  30.0 134.9 %collective-permute-start.3 = (bf16[192,768]{1,0:T(8,128)(2,1)S(1)}, bf16[192,768]{1,0:T(8,128)(2,1)S(1)}, u32[]{:S(2)}, u32[]{:S(2)}) collective-permute-start(bf16[192,768]{1,0:T(8,128)(2,1)S(1)} %bitcast.147), channel_id=1, source_target_pairs={{12,0},{16,4},{20,8},{24,12},{28,16},{32,20},{36,24},{40,28},{44,3... | collective-permute-start | bytes 884744 | tf_op jit(solution)/shard_map/ppermute | solution.py:15
  33.3 135.4 %collective-permute-start.2 = (bf16[192,768]{1,0:T(8,128)(2,1)S(1)}, bf16[192,768]{1,0:T(8,128)(2,1)S(1)}, u32[]{:S(2)}, u32[]{:S(2)}) collective-permute-start(bf16[192,768]{1,0:T(8,128)(2,1)S(1)} %bitcast.148), channel_id=1, source_target_pairs={{0,12},{4,16},{8,20},{12,24},{16,28},{20,32},{24,36},{28,40},{32,4... | collective-permute-start | bytes 884744 | tf_op jit(solution)/shard_map/ppermute | solution.py:15
  37.6 138.3 %collective-permute-start.1 = (bf16[192,768]{1,0:T(8,128)(2,1)S(1)}, bf16[192,768]{1,0:T(8,128)(2,1)S(1)}, u32[]{:S(2)}, u32[]{:S(2)}) collective-permute-start(bf16[192,768]{1,0:T(8,128)(2,1)S(1)} %bitcast.149), channel_id=1, source_target_pairs={{0,8},{4,12},{8,16},{12,20},{16,24},{20,28},{24,32},{28,36},{32,40... | collective-permute-start | bytes 884744 | tf_op jit(solution)/shard_map/ppermute | solution.py:15
  41.7 1.7 copy-start.3
  131.3 15.1 %copy-start.4 = (bf16[192,768]{1,0:T(8,128)(2,1)}, bf16[192,768]{1,0:T(8,128)(2,1)S(1)}, u32[]{:S(2)}) copy-start(bf16[192,768]{1,0:T(8,128)(2,1)S(1)} %collective-permute-done.5) | copy-start | bytes 884740
  131.3 47.3 %collective-permute-start = (bf16[192,768]{1,0:T(8,128)(2,1)S(1)}, bf16[192,768]{1,0:T(8,128)(2,1)}, u32[]{:S(2)}, u32[]{:S(2)}) collective-permute-start(bf16[192,768]{1,0:T(8,128)(2,1)S(1)} %bitcast.150), channel_id=1, source_target_pairs={{0,4},{4,8},{8,12},{12,16},{16,20},{20,24},{24,28},{28,32},{32,36}... | collective-permute-start | bytes 884744 | tf_op jit(solution)/shard_map/ppermute | solution.py:15
  146.4 41.0 %collective-permute-start.11 = (bf16[192,768]{1,0:T(8,128)(2,1)S(1)}, bf16[192,768]{1,0:T(8,128)(2,1)}, u32[]{:S(2)}, u32[]{:S(2)}) collective-permute-start(bf16[192,768]{1,0:T(8,128)(2,1)S(1)} %bitcast.151), channel_id=1, source_target_pairs={{4,0},{8,4},{12,8},{16,12},{20,16},{24,20},{28,24},{32,28},{36,32}... | collective-permute-start | bytes 884744 | tf_op jit(solution)/shard_map/ppermute | solution.py:15
  164.8 30.5 %collective-permute-start.10 = (bf16[192,768]{1,0:T(8,128)(2,1)S(1)}, bf16[192,768]{1,0:T(8,128)(2,1)}, u32[]{:S(2)}, u32[]{:S(2)}) collective-permute-start(bf16[192,768]{1,0:T(8,128)(2,1)S(1)} %bitcast.152), channel_id=1, source_target_pairs={{8,0},{12,4},{16,8},{20,12},{24,16},{28,20},{32,24},{36,28},{40,32... | collective-permute-start | bytes 884744 | tf_op jit(solution)/shard_map/ppermute | solution.py:15
  168.7 33.4 %collective-permute-start.9 = (bf16[192,768]{1,0:T(8,128)(2,1)S(1)}, bf16[192,768]{1,0:T(8,128)(2,1)}, u32[]{:S(2)}, u32[]{:S(2)}) collective-permute-start(bf16[192,768]{1,0:T(8,128)(2,1)S(1)} %bitcast.153), channel_id=1, source_target_pairs={{12,0},{16,4},{20,8},{24,12},{28,16},{32,20},{36,24},{40,28},{44,3... | collective-permute-start | bytes 884744 | tf_op jit(solution)/shard_map/ppermute | solution.py:15
  176.0 27.5 %collective-permute-start.8 = (bf16[192,768]{1,0:T(8,128)(2,1)S(1)}, bf16[192,768]{1,0:T(8,128)(2,1)}, u32[]{:S(2)}, u32[]{:S(2)}) collective-permute-start(bf16[192,768]{1,0:T(8,128)(2,1)S(1)} %bitcast.154), channel_id=1, source_target_pairs={{0,12},{4,16},{8,20},{12,24},{16,28},{20,32},{24,36},{28,40},{32,4... | collective-permute-start | bytes 884744 | tf_op jit(solution)/shard_map/ppermute | solution.py:15
  178.6 32.6 %collective-permute-start.6 = (bf16[192,768]{1,0:T(8,128)(2,1)S(1)}, bf16[192,768]{1,0:T(8,128)(2,1)S(1)}, u32[]{:S(2)}, u32[]{:S(2)}) collective-permute-start(bf16[192,768]{1,0:T(8,128)(2,1)S(1)} %bitcast.155), channel_id=1, source_target_pairs={{0,4},{4,8},{8,12},{12,16},{16,20},{20,24},{24,28},{28,32},{32,36}... | collective-permute-start | bytes 884744 | tf_op jit(solution)/shard_map/ppermute | solution.py:15
  183.4 1.2 copy-start.5
  187.5 25.2 %collective-permute-start.7 = (bf16[192,768]{1,0:T(8,128)(2,1)S(1)}, bf16[192,768]{1,0:T(8,128)(2,1)S(1)}, u32[]{:S(2)}, u32[]{:S(2)}) collective-permute-start(bf16[192,768]{1,0:T(8,128)(2,1)S(1)} %bitcast.156), channel_id=1, source_target_pairs={{0,8},{4,12},{8,16},{12,20},{16,24},{20,28},{24,32},{28,36},{32,40... | collective-permute-start | bytes 884744 | tf_op jit(solution)/shard_map/ppermute | solution.py:15
  218.2 0.7 copy-start.7
  218.2 43.1 %copy-start = (bf16[1,192,768]{2,1,0:T(8,128)(2,1)S(1)}, bf16[1,192,768]{2,1,0:T(8,128)(2,1)}, u32[]{:S(2)}) copy-start(bf16[1,192,768]{2,1,0:T(8,128)(2,1)} %param.10) | copy-start | bytes 884740
  262.4 14.9 %collective-permute-start.12 = (bf16[192,768]{1,0:T(8,128)(2,1)S(1)}, bf16[192,768]{1,0:T(8,128)(2,1)S(1)}, u32[]{:S(2)}, u32[]{:S(2)}) collective-permute-start(bf16[192,768]{1,0:T(8,128)(2,1)S(1)} %fusion.29), channel_id=1, source_target_pairs={{0,128},{128,256},{256,384},{384,0},{1,129},{129,257},{257,385},{3... | collective-permute-start | bytes 884744 | tf_op jit(solution)/shard_map/ppermute | solution.py:21
Sparse Core Ops, SparseCore 0:
  218.4 42.9 reduce-scatter.1
